TPU v7x, 256 devices: a whole 4x4x8 slice. The times are simulated.
256 devices in a mesh: group: 8 (over x, core), inner: 32 (over z, y).
Axes of the slice: x: 4, y: 4, z: 8, core: 2. Of those that a mesh axis runs over, the one named last changes fastest.
Arguments:
- flow_field: float32 [1536, 1536, 128], P('inner', 'group'), may hold values from -6 to 6
- sketch_rows: float32 [1536, 128], P('inner'), may hold values from -6 to 6
- sketch_cols: float32 [1536, 128], P('group'), may hold values from -6 to 6
- sketch_depth: float32 [128, 128], replicated, may hold values from -6 to 6
- bit_widths: int32 [2], replicated, may hold values from 6 to 8
- bin_edges: int32 [9], replicated, may hold values from -6 to 6, as said below
Outputs:
- basis_one: float32 [1536, 128], P('inner')
- basis_two: float32 [1536, 128], P('group')
- core: float32 [128, 128, 128], P('inner', 'group')
- residual: float32 [2, 128, 128, 128], P(None, 'inner', 'group')
- energy: float32 [2, 1536, 128], P(None, 'inner')
- histogram: float32 [2, 1536, 8], P(None, 'inner')
Inputs may be any that keep to these rules, and one draw needn't show every extreme that they name: `bin_edges`: strictly increasing; the first is -6 and the last 6.
All inputs are finite; a program needn't handle non-finite values.
Results may differ from a plain program's by a relative error of at most 0.0008.
Values sent between devices are 32-bit elements; how exact they have to be, the bound alone decides.
No kernel may reach another device: no remote copies, remote signals or barrier semaphores. Data moves between devices by JAX's collectives and lax.ppermute only.
A program may use at most 128 MiB of HBM per device.

v0:
```python
import math
import jax
import jax.numpy as jnp
from jax import lax
from jax.sharding import PartitionSpec as P

N1 = 1536
N2 = 1536
N3 = 128
R = 128
NEDGE = 9
NBINS = 8
precise = lax.Precision.HIGHEST
two_pi = 2.0 * 3.141592653589793
error_boost = 16.0


def gram_of(sketch):
    return jnp.dot(sketch.T, sketch, precision=precise)


def orthonormal_rows(sketch, gram_matrix):
    lower_factor = jnp.linalg.cholesky(gram_matrix)
    return jax.scipy.linalg.solve_triangular(lower_factor, sketch.T, lower=True).T


def soft_residual(core_values, step_size):
    return -jnp.sin(two_pi * core_values[None] / step_size[:, None, None, None]) / two_pi


def local(flow_field, sketch_rows, sketch_cols, sketch_depth, bit_widths, bin_edges):
    reduced = jnp.einsum("ijk,kr->ijr", flow_field, sketch_depth, precision=precise)
    mode_one = jnp.einsum("ijr,jr->ir", reduced, sketch_cols, precision=precise)
    mode_two = jnp.einsum("ijr,ir->jr", reduced, sketch_rows, precision=precise)
    mode_one = lax.psum(mode_one, "group")
    basis_one = orthonormal_rows(mode_one, lax.psum(gram_of(mode_one), "inner"))
    mode_two = lax.psum(mode_two, "inner")
    basis_two = orthonormal_rows(mode_two, lax.psum(gram_of(mode_two), "group"))
    along_two = jnp.einsum("ijk,js->isk", flow_field, basis_two, precision=precise)
    levels = jnp.exp2(bit_widths.astype(jnp.float32) - 1.0) - 1.0
    summed_two = lax.psum_scatter(along_two, "group", scatter_dimension=1, tiled=True)
    partial_rows = jnp.einsum("ir,isk->rsk", basis_one, summed_two, precision=precise)
    core_shard = lax.psum_scatter(partial_rows, "inner", scatter_dimension=0, tiled=True)
    peak = lax.pmax(jnp.max(jnp.abs(core_shard)), ("group", "inner"))
    residual_shard = soft_residual(core_shard, peak / levels)
    spread = lax.all_gather(residual_shard, "group", axis=2, tiled=True)
    mixed_core = jnp.einsum(
        "ir,brsk->bisk",
        basis_one,
        lax.all_gather(spread, "inner", axis=1, tiled=True),
        precision=precise,
    )
    error_scale = error_boost * math.sqrt(N1 * N2) / R
    field_error = error_scale * jnp.einsum(
        "bisk,js->bijk", mixed_core, basis_two, precision=precise
    )
    energy_part = jnp.sum(field_error * field_error, axis=2) / N2
    edge_values = bin_edges.astype(jnp.float32)
    ramp_part = jnp.stack(
        [
            jnp.sum(jnp.clip(field_error - edge_values[index_edge] + 0.5, 0.0, 1.0), axis=(2, 3))
            for index_edge in range(NEDGE)
        ],
        axis=-1,
    )
    energy, ramp_sums = lax.psum((energy_part, ramp_part), "group")
    histogram = (ramp_sums[..., :-1] - ramp_sums[..., 1:]) * (NBINS / (N2 * N3))
    return (basis_one, basis_two, core_shard, residual_shard, energy, histogram)


def solution(mesh):
    in_specs = (P("inner", "group", None), P("inner", None), P("group", None), P(), P(), P())
    out_specs = (
        P("inner", None),
        P("group", None),
        P("inner", "group", None),
        P(None, "inner", "group", None),
        P(None, "inner", None),
        P(None, "inner", None),
    )
    return jax.shard_map(local, mesh=mesh, in_specs=in_specs, out_specs=out_specs, check_vma=False)
```

profile of v0, /device:TPU:8, one launch (start us, length us, event | category | flops | bytes accessed | tf_op | source)
XLA Modules:
  0.0 863.6 jit_solution(15359649875850458368)
XLA Ops:
  7.2 0.8 copy-done
  8.0 7.1 multiply_reduce_fusion.2
  15.2 26.1 %psum.42 = f32[48,128]{0,1:T(8,128)S(1)} all-reduce(f32[48,128]{0,1:T(8,128)S(1)} %bitcast.98), channel_id=1, replica_groups=mesh['group'=8,'inner'=32] {'group'}, use_global_device_ids=true, to_apply=%region_0.0 | all-reduce | flops 6144 | bytes 49152 | tf_op jit(solution)/shard_map/psum | solution.py:35
  41.3 0.9 fusion.25
  42.2 2.8 multiply_reduce_fusion.1
  45.0 0.8 copy.39
  45.8 143.9 %all-reduce.7.cloned.1.call-done = (f32[128,128]{0,1:T(8,128)}, f32[192,128]{0,1:T(8,128)}) async-done(((f32[128,128]{0,1:T(8,128)}, f32[192,128]{0,1:T(8,128)}), (f32[128,128]{0,1:T(8,128)}, f32[192,128]{0,1:T(8,128)})) %all-reduce.7.cloned.1.call-update) | async-done | bytes 163856 | tf_op jit(solution)/shard_map/psum | solution.py:36
  189.7 1.9 fusion.26
  191.8 64.2 %all-reduce.5.cloned.1.call-done = f32[128,128]{0,1:T(8,128)} async-done(((f32[128,128]{0,1:T(8,128)}), f32[128,128]{0,1:T(8,128)}) %all-reduce.5.cloned.1.call-update) | async-done | bytes 65552 | tf_op jit(solution)/shard_map/psum | solution.py:38
  256.0 0.9 copy.22
  256.9 0.9 fusion.14
  257.8 11.7 %cholesky.55 = f32[128,128]{1,0:T(8,128)S(1)} custom-call(f32[128,128]{1,0:T(8,128)S(1)} %fusion.14), custom_call_target="Cholesky" | custom-call | tf_op jit(solution)/shard_map/jit(cholesky)/cholesky | solution.py:23
  270.2 0.7 fusion.11
  270.8 9.8 %custom-call.11 = f32[1,128,128]{1,2,0:T(8,128)S(1)} custom-call(f32[1,128,128]{2,1,0:T(8,128)S(1)} %fusion.11), custom_call_target="InvertDiagBlocksLowerTriangular" | custom-call | tf_op jit(solution)/shard_map/jit(_solve_triangular)/triangular_solve | solution.py:24
  280.6 1.3 fusion.12
  281.9 4.8 fusion.6
  286.8 3.5 copy.57
  290.7 11.7 %cholesky.44 = f32[128,128]{1,0:T(8,128)S(1)} custom-call(f32[128,128]{1,0:T(8,128)S(1)} %fusion.17), custom_call_target="Cholesky" | custom-call | tf_op jit(solution)/shard_map/jit(cholesky)/cholesky | solution.py:23
  303.1 0.7 fusion.10
  303.8 9.8 %custom-call.10 = f32[1,128,128]{1,2,0:T(8,128)S(1)} custom-call(f32[1,128,128]{2,1,0:T(8,128)S(1)} %fusion.10), custom_call_target="InvertDiagBlocksLowerTriangular" | custom-call | tf_op jit(solution)/shard_map/jit(_solve_triangular)/triangular_solve | solution.py:24
  313.9 14.2 %reduce-scatter.3.cloned.1.call-done = f32[48,16,128]{2,0,1:T(8,128)} async-done(((f32[48,128,128]{2,0,1:T(8,128)}), f32[48,16,128]{2,0,1:T(8,128)}) %reduce-scatter.3.cloned.1.call-update) | async-done | bytes 393232 | tf_op jit(solution)/shard_map/reduce_scatter | solution.py:41
  328.1 2.0 fusion.21
  330.1 1.6 copy.23
  331.8 215.3 %reduce-scatter.5.cloned.1.call-done = f32[4,16,128]{2,1,0:T(8,128)} async-done(((f32[128,16,128]{2,1,0:T(8,128)}), f32[4,16,128]{2,1,0:T(8,128)}) %reduce-scatter.5.cloned.1.call-update) | async-done | bytes 32784 | tf_op jit(solution)/shard_map/reduce_scatter | solution.py:43
  547.1 1.4 broadcast_multiply_fusion.2
  548.5 74.3 %pmax.7 = f32[]{:T(128)} all-reduce(f32[]{:T(128)} %get-tuple-element.34), channel_id=1, replica_groups=mesh['group'=8,'inner'=32] {'group','inner'}, use_global_device_ids=true, to_apply=%region_9.11 | all-reduce | flops 1 | bytes 8 | tf_op jit(solution)/shard_map/pmax | solution.py:44
  623.8 14.5 %all_gather.6 = f32[2,4,128,128]{3,2,1,0:T(8,128)} all-gather(f32[2,4,16,128]{3,2,1,0:T(8,128)S(1)} %fusion.9), channel_id=1, replica_groups=mesh['group'=8,'inner'=32] {'group'}, dimensions={2}, use_global_device_ids=true | all-gather | bytes 589824 | tf_op jit(solution)/shard_map/all_gather | solution.py:46
  638.3 0.7 fusion.24
  639.0 135.6 %all-gather.2.cloned.1.call-done = f32[2,128,128,128]{3,2,1,0:T(8,128)} async-done(((f32[2,4,128,128]{3,2,1,0:T(8,128)}), f32[2,128,128,128]{3,2,1,0:T(8,128)}) %all-gather.2.cloned.1.call-update) | async-done | bytes 16777232 | tf_op jit(solution)/shard_map/all_gather | solution.py:50
  774.6 22.9 %fusion = f32[2,128,128,48]{2,3,1,0:T(8,128)S(1)} fusion(f32[2,128,128,128]{3,2,1,0:T(8,128)} %all-gather.2.cloned.1.call-done, f32[128,48]{0,1:T(8,128)S(1)} %fusion.15), kind=kOutput, calls=%fused_computation | convolution fusion | flops 2415919104 | bytes 23093248 | tf_op jit(solution)/shard_map/ir,brsk->bisk/dot_general | solution.py:47
  797.5 32.9 %clamp_reduce_fusion = (f32[2,48]{1,0:T(2,128)S(1)}, f32[2,48]{1,0:T(2,128)S(1)}, f32[2,48]{1,0:T(2,128)S(1)}, f32[2,48]{1,0:T(2,128)S(1)}, f32[2,48]{1,0:T(2,12...) fusion(f32[]{:T(128)} %bitcast.39, f32[]{:T(128)} %bitcast.23, ...), kind=kOutput, calls=%fused_computation.2 | convolution fusion | flops 3715877888 | bytes 6442404 | tf_op jit(solution)/shard_map/bisk,js->bijk/dot_general | solution.py:54
  830.6 25.9 %all-reduce.1 = (f32[2,48,128]{2,1,0:T(8,128)}, f32[2,48,9]{1,0,2:T(2,128)S(1)}) all-reduce(f32[2,48,128]{2,1,0:T(8,128)S(1)} %broadcast_multiply_fusion.1, f32[2,48,9]{1,0,2:T(2,128)S(1)} %constant_dynamic-update-slice_fusion), channel_id=1, replica_groups=mesh['group'=8,'inner'=32] {'group'}, use_global_device_ids=true, to_apply=%region_11.13 | all-reduce | flops 13152 | bytes 105216 | tf_op jit(solution)/shard_map/psum | solution.py:66
  (48 shorter events, 4.2 us)
Async XLA Ops:
  7.2 0.8 copy-start
  7.2 35.0 %copy-start.5 = (f32[48,128]{1,0:T(8,128)S(1)}, f32[48,128]{1,0:T(8,128)}, u32[]{:S(2)}) copy-start(f32[48,128]{1,0:T(8,128)} %param.8) | copy-start | bytes 73732
  7.2 182.5 %all-reduce.7.cloned.1.call-start = ((), (), s32[]{:S(2)}) async-start(), calls=%async_computation.6 | async-start | bytes 393216 | tf_op jit(solution)/shard_map/psum | solution.py:36
  45.7 210.2 %all-reduce.5.cloned.1.call-start = ((), (), s32[]{:S(2)}) async-start(), calls=%async_computation.2 | async-start | bytes 131072 | tf_op jit(solution)/shard_map/psum | solution.py:38
  189.7 100.9 %copy-start.3 = (f32[128,128]{0,1:T(8,128)S(1)}, f32[128,128]{0,1:T(8,128)}, u32[]{:S(2)}) copy-start(f32[128,128]{0,1:T(8,128)} %get-tuple-element.29) | copy-start | bytes 196612
  191.6 136.5 %reduce-scatter.3.cloned.1.call-start = ((), (), s32[]{:S(2)}) async-start(), calls=%async_computation.3 | async-start | bytes 3538944 | tf_op jit(solution)/shard_map/reduce_scatter | solution.py:41
  281.9 515.6 %copy-start.1 = (f32[128,192]{0,1:T(8,128)}, f32[128,192]{0,1:T(8,128)S(1)}, u32[]{:S(2)}) copy-start(f32[128,192]{0,1:T(8,128)S(1)} %fusion.12) | copy-start | bytes 294916
  281.9 340.9 %copy-start.6 = (s32[2]{0:T(128)S(1)}, s32[2]{0:T(128)}, u32[]{:S(2)}) copy-start(s32[2]{0:T(128)} %param.11) | copy-start | bytes 28
  286.8 351.5 %copy-start.7 = (s32[9]{0:T(128)S(1)}, s32[9]{0:T(128)}, u32[]{:S(2)}) copy-start(s32[9]{0:T(128)} %param.12) | copy-start | bytes 112
  290.3 256.8 %reduce-scatter.5.cloned.1.call-start = ((), (), s32[]{:S(2)}) async-start(), calls=%async_computation.4 | async-start | bytes 1081344 | tf_op jit(solution)/shard_map/reduce_scatter | solution.py:43
  313.9 483.7 %copy-start.4 = (f32[128,48]{0,1:T(8,128)}, f32[128,48]{0,1:T(8,128)S(1)}, u32[]{:S(2)}) copy-start(f32[128,48]{0,1:T(8,128)S(1)} %fusion.15) | copy-start | bytes 73732
  331.7 442.9 %all-gather.2.cloned.1.call-start = ((), (), s32[]{:S(2)}) async-start(), calls=%async_computation.5 | async-start | bytes 17301504 | tf_op jit(solution)/shard_map/all_gather | solution.py:50
  623.8 173.7 %copy-start.2 = (f32[2,4,16,128]{3,2,1,0:T(8,128)}, f32[2,4,16,128]{3,2,1,0:T(8,128)S(1)}, u32[]{:S(2)}) copy-start(f32[2,4,16,128]{3,2,1,0:T(8,128)S(1)} %fusion.9) | copy-start | bytes 196612
Sparse Core Ops, SparseCore 0:
  45.9 143.7 all-reduce.6
  192.5 63.3 all-reduce.4
  290.4 37.5 reduce-scatter.2
  332.3 214.7 reduce-scatter.4
  638.4 136.1 all-gather.1
where the time goes:
time: 864 us
  waiting for transfers between devices  573 us (66%)
  blocking collectives  141 us (16%)
  matrix products  74.1 us (9%)
  other arithmetic  51.7 us (6%)
  between operations  14 us (2%)
  local copies, waits for them, and re-layouts  9.15 us (1%)
    reduce_scatter x1, waiting for transfers between devices, local(): lax.psum_scatter(partial_rows, 'inner', scatter_dimension=0, tiled=True)  215 us
    psum x1, waiting for transfers between devices, local(): basis_one = orthonormal_rows(mode_one, lax.psum(gram_of(mode_one), 'inner'))  144 us
    all_gather x1, waiting for transfers between devices, local(): lax.all_gather(spread, 'inner', axis=1, tiled=True)  136 us
    pmax x1, blocking collectives, local(): peak = lax.pmax(jnp.max(jnp.abs(core_shard)), ('group', 'inner'))  74.3 us
    psum x1, waiting for transfers between devices, local(): basis_two = orthonormal_rows(mode_two, lax.psum(gram_of(mode_two), 'group'))  64.2 us
    dot_general x1, matrix products, local(): jnp.einsum('bisk,js->bijk', mixed_core, basis_two, precision=precise)  32.9 us
    psum x1, blocking collectives, local(): mode_one = lax.psum(mode_one, 'group')  26.1 us
    psum x1, blocking collectives, local(): energy, ramp_sums = lax.psum((energy_part, ramp_part), 'group')  25.9 us
  transfers between devices with their start and end apart: 5, of which 5 were waited for; matrix products, arithmetic and copies ran while one was open for 3% of the time, Pallas kernels for 0%

commit v1 on v0

--- a/solution.py
+++ b/solution.py
@@ -35,7 +35,9 @@
     mode_one = lax.psum(mode_one, "group")
     basis_one = orthonormal_rows(mode_one, lax.psum(gram_of(mode_one), "inner"))
     mode_two = lax.psum(mode_two, "inner")
-    basis_two = orthonormal_rows(mode_two, lax.psum(gram_of(mode_two), "group"))
+    basis_two = orthonormal_rows(
+        mode_two, jnp.sum(lax.all_gather(gram_of(mode_two), "group"), axis=0)
+    )
     along_two = jnp.einsum("ijk,js->isk", flow_field, basis_two, precision=precise)
     levels = jnp.exp2(bit_widths.astype(jnp.float32) - 1.0) - 1.0
     summed_two = lax.psum_scatter(along_two, "group", scatter_dimension=1, tiled=True)

time: 864 us -> 810 us (0.938)
  waiting for transfers between devices: 573 us -> 508 us
  blocking collectives: 141 us -> 154 us
    psum x1 -> x0, waiting for transfers between devices: 64.2 us -> none  [local(): basis_two = orthonormal_rows(mode_two, lax.psum(gram_of(mode_two), 'group'))]
    all_gather x0 -> x1, blocking collectives: none -> 13.6 us  [local(): lax.all_gather(gram_of(mode_two), 'group')]
  transfers between devices with their start and end apart: 5 -> 4, of which waited for: 5 -> 4; matrix products, arithmetic and copies ran while one was open for 3% -> 3% of each run, Pallas kernels for 0% -> 0%
where the time goes in v1:
time: 810 us
  waiting for transfers between devices  508 us (63%)
  blocking collectives  154 us (19%)
  matrix products  73.5 us (9%)
  other arithmetic  50.9 us (6%)
  between operations  14 us (2%)
  local copies, waits for them, and re-layouts  8.31 us (1%)
    reduce_scatter x1, waiting for transfers between devices, local(): lax.psum_scatter(partial_rows, 'inner', scatter_dimension=0, tiled=True)  215 us
    psum x1, waiting for transfers between devices, local(): basis_one = orthonormal_rows(mode_one, lax.psum(gram_of(mode_one), 'inner'))  144 us
    all_gather x1, waiting for transfers between devices, local(): lax.all_gather(spread, 'inner', axis=1, tiled=True)  136 us
    pmax x1, blocking collectives, local(): peak = lax.pmax(jnp.max(jnp.abs(core_shard)), ('group', 'inner'))  74.3 us
    dot_general x1, matrix products, local(): jnp.einsum('bisk,js->bijk', mixed_core, basis_two, precision=precise)  32.9 us
    psum x1, blocking collectives, local(): mode_one = lax.psum(mode_one, 'group')  26.1 us
    psum x1, blocking collectives, local(): energy, ramp_sums = lax.psum((energy_part, ramp_part), 'group')  25.9 us
    another operation x6, other arithmetic, orthonormal_rows(): lower_factor = jnp.linalg.cholesky(gram_matrix)  24.8 us
  transfers between devices with their start and end apart: 4, of which 4 were waited for; matrix products, arithmetic and copies ran while one was open for 3% of the time, Pallas kernels for 0%

profile of v1, /device:TPU:8, one launch (start us, length us, event | category | flops | bytes accessed | tf_op | source)
XLA Modules:
  0.0 809.5 jit_solution(15507771966093478503)
XLA Ops:
  7.2 0.8 copy-done
  8.0 7.1 multiply_reduce_fusion.2
  15.2 26.1 %psum.35 = f32[48,128]{0,1:T(8,128)S(1)} all-reduce(f32[48,128]{0,1:T(8,128)S(1)} %bitcast.100), channel_id=1, replica_groups=mesh['group'=8,'inner'=32] {'group'}, use_global_device_ids=true, to_apply=%region_0.0 | all-reduce | flops 6144 | bytes 49152 | tf_op jit(solution)/shard_map/psum | solution.py:35
  41.3 0.9 fusion.25
  42.2 2.8 multiply_reduce_fusion.1
  45.0 0.8 copy.37
  45.8 143.9 %all-reduce.4.cloned.1.call-done = (f32[128,128]{0,1:T(8,128)}, f32[192,128]{0,1:T(8,128)}) async-done(((f32[128,128]{0,1:T(8,128)}, f32[192,128]{0,1:T(8,128)}), (f32[128,128]{0,1:T(8,128)}, f32[192,128]{0,1:T(8,128)})) %all-reduce.4.cloned.1.call-update) | async-done | bytes 163856 | tf_op jit(solution)/shard_map/psum | solution.py:36
  189.7 1.3 fusion.26
  190.9 13.6 %all-gather = f32[1024,128]{1,0:T(8,128)S(1)} all-gather(f32[128,128]{1,0:T(8,128)S(1)} %fusion.26), channel_id=2, replica_groups=mesh['group'=8,'inner'=32] {'group'}, dimensions={0}, use_global_device_ids=true | all-gather | bytes 589824 | tf_op jit(solution)/shard_map/all_gather | solution.py:39
  204.7 11.7 %cholesky.55 = f32[128,128]{1,0:T(8,128)S(1)} custom-call(f32[128,128]{1,0:T(8,128)S(1)} %fusion.14), custom_call_target="Cholesky" | custom-call | tf_op jit(solution)/shard_map/jit(cholesky)/cholesky | solution.py:23
  216.4 0.6 compare_reduce_fusion
  217.1 0.7 fusion.11
  217.7 9.8 %custom-call.11 = f32[1,128,128]{1,2,0:T(8,128)S(1)} custom-call(f32[1,128,128]{2,1,0:T(8,128)S(1)} %fusion.11), custom_call_target="InvertDiagBlocksLowerTriangular" | custom-call | tf_op jit(solution)/shard_map/jit(_solve_triangular)/triangular_solve | solution.py:24
  227.5 1.3 fusion.12
  228.8 4.8 fusion.6
  233.7 3.5 copy.54
  237.6 11.7 %cholesky.44 = f32[128,128]{1,0:T(8,128)S(1)} custom-call(f32[128,128]{1,0:T(8,128)S(1)} %fusion.17), custom_call_target="Cholesky" | custom-call | tf_op jit(solution)/shard_map/jit(cholesky)/cholesky | solution.py:23
  250.0 0.7 fusion.10
  250.7 9.8 %custom-call.10 = f32[1,128,128]{1,2,0:T(8,128)S(1)} custom-call(f32[1,128,128]{2,1,0:T(8,128)S(1)} %fusion.10), custom_call_target="InvertDiagBlocksLowerTriangular" | custom-call | tf_op jit(solution)/shard_map/jit(_solve_triangular)/triangular_solve | solution.py:24
  260.8 13.2 %reduce-scatter.3.cloned.1.call-done = f32[48,16,128]{2,0,1:T(8,128)} async-done(((f32[48,128,128]{2,0,1:T(8,128)}), f32[48,16,128]{2,0,1:T(8,128)}) %reduce-scatter.3.cloned.1.call-update) | async-done | bytes 393232 | tf_op jit(solution)/shard_map/reduce_scatter | solution.py:43
  274.0 2.0 fusion.21
  276.0 1.6 copy.21
  277.7 215.3 %reduce-scatter.5.cloned.1.call-done = f32[4,16,128]{2,1,0:T(8,128)} async-done(((f32[128,16,128]{2,1,0:T(8,128)}), f32[4,16,128]{2,1,0:T(8,128)}) %reduce-scatter.5.cloned.1.call-update) | async-done | bytes 32784 | tf_op jit(solution)/shard_map/reduce_scatter | solution.py:45
  493.0 1.4 broadcast_multiply_fusion.2
  494.4 74.3 %pmax.7 = f32[]{:T(128)} all-reduce(f32[]{:T(128)} %get-tuple-element.34), channel_id=1, replica_groups=mesh['group'=8,'inner'=32] {'group','inner'}, use_global_device_ids=true, to_apply=%region_9.11 | all-reduce | flops 1 | bytes 8 | tf_op jit(solution)/shard_map/pmax | solution.py:46
  568.7 0.7 add_divide_fusion
  569.7 14.5 %all_gather.14 = f32[2,4,128,128]{3,2,1,0:T(8,128)} all-gather(f32[2,4,16,128]{3,2,1,0:T(8,128)S(1)} %fusion.9), channel_id=1, replica_groups=mesh['group'=8,'inner'=32] {'group'}, dimensions={2}, use_global_device_ids=true | all-gather | bytes 589824 | tf_op jit(solution)/shard_map/all_gather | solution.py:48
  584.2 0.7 fusion.24
  584.9 135.7 %all-gather.3.cloned.1.call-done = f32[2,128,128,128]{3,2,1,0:T(8,128)} async-done(((f32[2,4,128,128]{3,2,1,0:T(8,128)}), f32[2,128,128,128]{3,2,1,0:T(8,128)}) %all-gather.3.cloned.1.call-update) | async-done | bytes 16777232 | tf_op jit(solution)/shard_map/all_gather | solution.py:52
  720.5 22.9 %fusion = f32[2,128,128,48]{2,3,1,0:T(8,128)S(1)} fusion(f32[2,128,128,128]{3,2,1,0:T(8,128)} %all-gather.3.cloned.1.call-done, f32[128,48]{0,1:T(8,128)S(1)} %fusion.15), kind=kOutput, calls=%fused_computation | convolution fusion | flops 2415919104 | bytes 23093248 | tf_op jit(solution)/shard_map/ir,brsk->bisk/dot_general | solution.py:49
  743.4 32.9 %clamp_reduce_fusion = (f32[2,48]{1,0:T(2,128)S(1)}, f32[2,48]{1,0:T(2,128)S(1)}, f32[2,48]{1,0:T(2,128)S(1)}, f32[2,48]{1,0:T(2,128)S(1)}, f32[2,48]{1,0:T(2,12...) fusion(f32[]{:T(128)} %bitcast.40, f32[]{:T(128)} %bitcast.24, ...), kind=kOutput, calls=%fused_computation.2 | convolution fusion | flops 3715877888 | bytes 6442404 | tf_op jit(solution)/shard_map/bisk,js->bijk/dot_general | solution.py:56
  776.5 25.9 %all-reduce.1 = (f32[2,48,128]{2,1,0:T(8,128)}, f32[2,48,9]{1,0,2:T(2,128)S(1)}) all-reduce(f32[2,48,128]{2,1,0:T(8,128)S(1)} %broadcast_multiply_fusion.1, f32[2,48,9]{1,0,2:T(2,128)S(1)} %constant_dynamic-update-slice_fusion), channel_id=1, replica_groups=mesh['group'=8,'inner'=32] {'group'}, use_global_device_ids=true, to_apply=%region_11.13 | all-reduce | flops 13152 | bytes 105216 | tf_op jit(solution)/shard_map/psum | solution.py:68
  (47 shorter events, 2.8 us)
Async XLA Ops:
  7.2 0.8 copy-start
  7.2 35.0 %copy-start.5 = (f32[48,128]{1,0:T(8,128)S(1)}, f32[48,128]{1,0:T(8,128)}, u32[]{:S(2)}) copy-start(f32[48,128]{1,0:T(8,128)} %param.8) | copy-start | bytes 73732
  7.2 182.5 %all-reduce.4.cloned.1.call-start = ((), (), s32[]{:S(2)}) async-start(), calls=%async_computation.5 | async-start | bytes 393216 | tf_op jit(solution)/shard_map/psum | solution.py:36
  45.7 228.3 %reduce-scatter.3.cloned.1.call-start = ((), (), s32[]{:S(2)}) async-start(), calls=%async_computation.2 | async-start | bytes 3538944 | tf_op jit(solution)/shard_map/reduce_scatter | solution.py:43
  204.5 33.0 %copy-start.3 = (f32[128,128]{0,1:T(8,128)S(1)}, f32[128,128]{0,1:T(8,128)}, u32[]{:S(2)}) copy-start(f32[128,128]{0,1:T(8,128)} %get-tuple-element.29) | copy-start | bytes 196612
  228.8 514.6 %copy-start.1 = (f32[128,192]{0,1:T(8,128)}, f32[128,192]{0,1:T(8,128)S(1)}, u32[]{:S(2)}) copy-start(f32[128,192]{0,1:T(8,128)S(1)} %fusion.12) | copy-start | bytes 294916
  228.8 339.8 %copy-start.6 = (s32[2]{0:T(128)S(1)}, s32[2]{0:T(128)}, u32[]{:S(2)}) copy-start(s32[2]{0:T(128)} %param.11) | copy-start | bytes 28
  233.7 350.4 %copy-start.7 = (s32[9]{0:T(128)S(1)}, s32[9]{0:T(128)}, u32[]{:S(2)}) copy-start(s32[9]{0:T(128)} %param.12) | copy-start | bytes 112
  237.2 255.8 %reduce-scatter.5.cloned.1.call-start = ((), (), s32[]{:S(2)}) async-start(), calls=%async_computation.3 | async-start | bytes 1081344 | tf_op jit(solution)/shard_map/reduce_scatter | solution.py:45
  260.8 482.6 %copy-start.4 = (f32[128,48]{0,1:T(8,128)}, f32[128,48]{0,1:T(8,128)S(1)}, u32[]{:S(2)}) copy-start(f32[128,48]{0,1:T(8,128)S(1)} %fusion.15) | copy-start | bytes 73732
  277.7 442.8 %all-gather.3.cloned.1.call-start = ((), (), s32[]{:S(2)}) async-start(), calls=%async_computation.4 | async-start | bytes 17301504 | tf_op jit(solution)/shard_map/all_gather | solution.py:52
  569.6 173.8 %copy-start.2 = (f32[2,4,16,128]{3,2,1,0:T(8,128)}, f32[2,4,16,128]{3,2,1,0:T(8,128)S(1)}, u32[]{:S(2)}) copy-start(f32[2,4,16,128]{3,2,1,0:T(8,128)S(1)} %fusion.9) | copy-start | bytes 196612
Sparse Core Ops, SparseCore 0:
  45.9 143.7 all-reduce.3
  237.3 36.6 reduce-scatter.2
  278.4 214.5 reduce-scatter.4
  584.3 136.2 all-gather.2
